TPU v7x, 32 devices: a whole 2x2x4 slice. The times are simulated.
32 devices in a mesh: walk: 4 (over x, core), chol: 8 (over z, y).
Axes of the slice: x: 2, y: 2, z: 4, core: 2. Of those that a mesh axis runs over, the one named last changes fastest.
Arguments:
- old_walkers: bfloat16 [96, 2048, 128], P(('walk', 'chol'))
- half_chol: bfloat16 [16, 128, 2048], P('chol'), may hold values from -0.1875 to 0.1875
- parent: int32 [192], P(('walk', 'chol')), may hold values from -1 to 11, as said below
- field: float32 [192, 2048], P(('walk', 'chol')), may hold values from -0.8 to 0.8
Outputs:
- new_walkers: bfloat16 [192, 2048, 128], P(('walk', 'chol'))
- energy: float32 [192], P(('walk', 'chol'))
Inputs may be any that keep to these rules, and one draw needn't show every extreme that they name: `parent`: the 4 devices that share an index of chol form a column. On each device the live slots (value >= 0) come first among its 6 slots, the rest hold -1. Each column has exactly 12 live slots, every device of it at least one, and some device of it has all 6 slots live. A live value m names the walker that the column's walk index m // 3 holds as its local walker m % 3.
All inputs are finite; a program needn't handle non-finite values.
Results may differ from a plain program's by a relative error of at most 0.0062.
Values may be sent and summed in bfloat16 or wider, within the bound.
No kernel may reach another device: no remote copies, remote signals or barrier semaphores. Data moves between devices by JAX's collectives and lax.ppermute only.
A program may use at most 192 MiB of HBM per device.

v0:
```python
import jax
import jax.numpy as jnp
from jax import lax
from jax.sharding import PartitionSpec as P

ITERS = 3


def green_half(walkers):
    widened = walkers.astype(jnp.float32)
    electrons = walkers.shape[2]
    intersection = widened[:, :electrons, :]
    identity = jnp.eye(electrons, dtype=jnp.float32)
    diagonal = jnp.diagonal(intersection, axis1=1, axis2=2)
    inverse = identity[None, :, :] / diagonal[:, None, :]
    for sweep in range(ITERS):
        product = jnp.einsum("wij,wjk->wik", intersection, inverse, precision=lax.Precision.HIGHEST)
        inverse = jnp.einsum(
            "wij,wjk->wik",
            inverse,
            2.0 * identity[None, :, :] - product,
            precision=lax.Precision.HIGHEST,
        )
    theta = jnp.einsum("wnk,wkj->wnj", widened, inverse, precision=lax.Precision.HIGHEST)
    return theta.astype(jnp.bfloat16)


def block_energy(theta, vectors):
    blocks = jnp.einsum("gin,wnj->wgij", vectors, theta, preferred_element_type=jnp.float32)
    traces = jnp.einsum("wgii->wg", blocks)
    crossed = jnp.sum(blocks * jnp.swapaxes(blocks, 2, 3), axis=(2, 3))
    return 0.5 * jnp.sum(traces * traces - crossed, axis=1)


def body(old_walkers, half_chol, parent, field):
    slot_dev = parent.shape[0]
    column = lax.all_gather(old_walkers, "walk", axis=0, tiled=True)
    living = parent >= 0
    source = jnp.maximum(parent, 0)
    kicked = (jnp.exp(field)[:, :, None] * column[source].astype(jnp.float32)).astype(jnp.bfloat16)
    new_walkers = jnp.where(living[:, None, None], kicked, jnp.zeros_like(kicked))
    theta = green_half(kicked)
    energy = jnp.zeros((slot_dev,), jnp.float32) + block_energy(
        theta, lax.all_gather(half_chol, "chol", axis=0, tiled=True)
    )
    energy = jnp.where(living, energy, 0.0)
    return (new_walkers, energy)


def solution(mesh):
    return jax.shard_map(
        body,
        mesh=mesh,
        in_specs=(
            P(("walk", "chol"), None, None),
            P("chol", None, None),
            P(("walk", "chol")),
            P(("walk", "chol"), None),
        ),
        out_specs=(P(("walk", "chol"), None, None), P(("walk", "chol"))),
        check_vma=False,
    )
```

profile of v0, /device:TPU:0, one launch (start us, length us, event | category | flops | bytes accessed | tf_op | source)
XLA Modules:
  0.0 217.5 jit_solution(15850261391445615935)
XLA Ops:
  7.2 0.0 all-gather.3.cloned.1.call-start
  7.2 0.7 all-gather.3.cloned.1.call-update
  7.9 0.0 all-gather.5.cloned.1.call-start
  7.9 0.7 all-gather.5.cloned.1.call-update
  8.6 0.9 exp.3
  9.5 0.7 broadcast_maximum_fusion
  10.2 0.6 iota_compare_fusion.1
  10.8 0.6 fusion.15
  11.4 0.7 fusion.16
  12.1 0.7 broadcast_compare_fusion
  12.7 45.9 %all-gather.3.cloned.1.call-done = bf16[12,2048,128]{2,1,0:T(8,128)(2,1)} async-done(((bf16[3,2048,128]{2,1,0:T(8,128)(2,1)}), bf16[12,2048,128]{2,1,0:T(8,128)(2,1)}) %all-gather.3.cloned.1.call-update) | async-done | bytes 6291472 | tf_op jit(solution)/shard_map/all_gather | solution.py:37
  58.7 5.5 %gather_fusion = bf16[6,2048,128]{2,1,0:T(8,128)(2,1)} fusion(bf16[12,2048,128]{2,1,0:T(8,128)(2,1)} %all-gather.3.cloned.1.call-done, s32[1024]{0:T(1024)S(1)} %pad_clamp_fusion), kind=kCustom, calls=%fused_computation | custom fusion | bytes 6291480 | tf_op jit(solution)/shard_map/gather | solution.py:40
  64.2 5.1 %broadcast_select_fusion = (bf16[6,2048,128]{2,1,0:T(8,128)(2,1)}, bf16[6,2048,128]{2,1,0:T(8,128)(2,1)S(1)}) fusion(pred[6]{0:T(512)(128)(4,1)S(1)} %broadcast_compare_fusion, bf16[6,2048,128]{2,1,0:T(8,128)(2,1)} %gather_fusion, f32[6,2048]{1,0:T(8,128)S(1)} %exp.3), kind=kLoop, calls=%fused_computation.11 | loop fusion | flops 6291456 | bytes 9486342 | tf_op jit(solution)/shard_map/jit(_where)/select_n | solution.py:41
  69.3 4.7 %copy.17 = f32[6,128,128]{0,2,1:T(8,128)} copy(f32[6,128,128]{2,1,0:T(8,128)S(1)} %slice_convert_fusion) | data formatting | bytes 786432 | tf_op jit(solution)/shard_map/slice | solution.py:12
  74.0 0.0 copy-start
  74.0 1.8 gather_fusion.1
  75.8 0.1 copy.18
  75.8 1.3 convolution_subtract_fusion.2
  77.1 1.4 fusion.5
  78.5 0.0 copy-done
  78.5 0.3 convolution_subtract_fusion.1
  78.9 0.5 fusion.17
  79.4 0.3 convolution_subtract_fusion
  79.7 0.5 fusion.18
  80.3 4.0 %convolution_convert_fusion = bf16[6,2048,128]{2,1,0:T(8,128)(2,1)} fusion(bf16[6,2048,128]{2,1,0:T(8,128)(2,1)S(1)} %get-tuple-element.7, f32[6,128,128]{2,1,0:T(8,128)S(1)} %fusion.18), kind=kOutput, calls=%fused_computation.9 | convolution fusion | flops 2417491968 | bytes 6684672 | tf_op jit(solution)/shard_map/wnk,wkj->wnj/dot_general | solution.py:24
  84.2 101.5 %all-gather.5.cloned.1.call-done = bf16[16,128,2048]{2,1,0:T(8,128)(2,1)} async-done(((bf16[2,128,2048]{2,1,0:T(8,128)(2,1)}), bf16[16,128,2048]{2,1,0:T(8,128)(2,1)}) %all-gather.5.cloned.1.call-update) | async-done | bytes 8388624 | tf_op jit(solution)/shard_map/all_gather | solution.py:44
  185.8 11.7 %fusion = f32[6,128,16,128]{3,1,2,0:T(8,128)} fusion(bf16[16,128,2048]{2,1,0:T(8,128)(2,1)} %all-gather.5.cloned.1.call-done, bf16[6,2048,128]{2,1,0:T(8,128)(2,1)} %convolution_convert_fusion), kind=kOutput, calls=%fused_computation.2 | convolution fusion | flops 6442450944 | bytes 17825792 | tf_op jit(solution)/shard_map/gin,wnj->wgij/dot_general | solution.py:29
  197.5 0.0 copy-start.1
  197.5 6.6 %copy.20 = f32[6,128,16,128]{1,3,2,0:T(8,128)} copy(f32[6,128,16,128]{3,1,2,0:T(8,128)} %fusion) | data formatting | bytes 12582912 | tf_op jit(solution)/shard_map/gin,wnj->wgij/dot_general | solution.py:29
  204.1 0.0 copy-done.1
  204.1 0.0 copy-start.2
  204.1 5.9 %fusion.3 = (f32[6,16]{1,0:T(8,128)S(1)}, f32[6,16]{1,0:T(8,128)S(1)}) fusion(f32[6,128,16,128]{1,3,2,0:T(8,128)} %copy.20, pred[128,128]{1,0:T(8,128)(4,1)S(1)} %copy-done.1, f32[6,128,16,128]{3,1,2,0:T(8,128)} %fusion), kind=kLoop, calls=%fused_computation.7 | loop fusion | flops 6291264 | bytes 12600064 | tf_op jit(solution)/shard_map/wgii->wg/reduce_sum | solution.py:30
  210.0 0.1 subtract_reduce_fusion
  210.1 0.0 copy-done.2
  210.1 0.5 multiply_select_fusion
  (3 shorter events, 0.0 us)
Async XLA Ops:
  7.2 51.5 %all-gather.3.cloned.1.call-start = ((), (), s32[]{:S(2)}) async-start(), calls=%async_computation | async-start | bytes 7864320 | tf_op jit(solution)/shard_map/all_gather | solution.py:37
  7.9 177.9 %all-gather.5.cloned.1.call-start = ((), (), s32[]{:S(2)}) async-start(), calls=%async_computation.1 | async-start | bytes 9437184 | tf_op jit(solution)/shard_map/all_gather | solution.py:44
  74.0 4.5 %copy-start = (f32[128,128]{1,0:T(8,128)S(1)}, f32[128,128]{1,0:T(8,128)}, u32[]{:S(2)}) copy-start(f32[128,128]{1,0:T(8,128)} %fusion.15) | copy-start | bytes 196612
  197.5 6.6 %copy-start.1 = (pred[128,128]{1,0:T(8,128)(4,1)S(1)}, pred[128,128]{1,0:T(8,128)(4,1)}, u32[]{:S(2)}) copy-start(pred[128,128]{1,0:T(8,128)(4,1)} %iota_compare_fusion.1) | copy-start | bytes 49156
  204.1 6.0 %copy-start.2 = (s32[6]{0:T(128)S(1)}, s32[6]{0:T(128)}, u32[]{:S(2)}) copy-start(s32[6]{0:T(128)} %param.6) | copy-start | bytes 76
Sparse Core Ops, SparseCore 0:
  9.6 49.0 all-gather.2
  60.8 124.9 all-gather.4
where the time goes:
time: 218 us; the launch traced here: 217 us
  waiting for transfers between devices  149 us (68%)
  matrix products  20.1 us (9%)
  local copies, waits for them, and re-layouts  19.5 us (9%)
  other arithmetic  14.8 us (7%)
  between operations  14.1 us (6%)
    all_gather x1, waiting for transfers between devices, body(): lax.all_gather(half_chol, 'chol', axis=0, tiled=True)  102 us
    all_gather x1, waiting for transfers between devices, body(): column = lax.all_gather(old_walkers, 'walk', axis=0, tiled=True)  45.9 us
    dot_general x1, matrix products, block_energy(): jnp.einsum('gin,wnj->wgij', vectors, theta, preferred_element_type=jnp.fl...  11.7 us
    dot_general x1, local copies, waits for them, and re-layouts, block_energy(): jnp.einsum('gin,wnj->wgij', vectors, theta, preferred_element_type=jnp.fl...  6.6 us
    reduce_sum x1, other arithmetic, block_energy(): traces = jnp.einsum('wgii->wg', blocks)  5.87 us
    gather x1, local copies, waits for them, and re-layouts, body(): column[source].astype(jnp.float32)  5.5 us
    select_n x1, other arithmetic, body(): jnp.where(living[:, None, None], kicked, jnp.zeros_like(kicked))  5.09 us
    slice x1, local copies, waits for them, and re-layouts, green_half(): intersection = widened[:, :electrons, :]  4.72 us
  transfers between devices with their start and end apart: 2, of which 2 were waited for; matrix products, arithmetic and copies ran while one was open for 14% of the time, Pallas kernels for 0%

commit v1 on v0

--- a/solution.py
+++ b/solution.py
@@ -34,7 +34,12 @@
 
 def body(old_walkers, half_chol, parent, field):
     slot_dev = parent.shape[0]
-    column = lax.all_gather(old_walkers, "walk", axis=0, tiled=True)
+    ring = [old_walkers]
+    for hop in range(3):
+        ring.append(lax.ppermute(ring[-1], "walk", [(dev, (dev + 1) % 4) for dev in range(4)]))
+    column = jnp.roll(
+        jnp.concatenate(ring[::-1], axis=0), (lax.axis_index("walk") + 1) * ring[0].shape[0], axis=0
+    )
     living = parent >= 0
     source = jnp.maximum(parent, 0)
     kicked = (jnp.exp(field)[:, :, None] * column[source].astype(jnp.float32)).astype(jnp.bfloat16)

time: 218 us -> 170 us (0.78)
  waiting for transfers between devices: 149 us -> 88.3 us
  local copies, waits for them, and re-layouts: 19.5 us -> 29.9 us
    all_gather x1, waiting for transfers between devices: 102 us -> 31.4 us  [body(): lax.all_gather(half_chol, 'chol', axis=0, tiled=True)]
    ppermute x0 -> x3, waiting for transfers between devices: none -> 56.2 us  [body(): lax.ppermute(ring[-1], 'walk', [(dev, (dev + 1) % 4) for dev in range(4)])]
    all_gather x1 -> x0, waiting for transfers between devices: 45.9 us -> none  [body(): column = lax.all_gather(old_walkers, 'walk', axis=0, tiled=True)]
    unnamed x6 -> x13, local copies, waits for them, and re-layouts: 0.01 us -> 6.99 us
    dynamic_slice x0 -> x1, local copies, waits for them, and re-layouts: none -> 3.14 us  [body(): jnp.roll(jnp.concatenate(ring[::-1], axis=0), (lax.axis_index('walk') + 1...]
  transfers between devices with their start and end apart: 2 -> 4, of which waited for: 2 -> 4; matrix products, arithmetic and copies ran while one was open for 14% -> 25% of each run, Pallas kernels for 0% -> 0%
where the time goes in v1:
time: 170 us
  waiting for transfers between devices  88.3 us (52%)
  local copies, waits for them, and re-layouts  29.9 us (18%)
  matrix products  21.7 us (13%)
  other arithmetic  14.8 us (9%)
  between operations  14.2 us (8%)
    ppermute x3, waiting for transfers between devices, body(): lax.ppermute(ring[-1], 'walk', [(dev, (dev + 1) % 4) for dev in range(4)])  56.2 us
    all_gather x1, waiting for transfers between devices, body(): lax.all_gather(half_chol, 'chol', axis=0, tiled=True)  31.4 us
    dot_general x1, matrix products, block_energy(): jnp.einsum('gin,wnj->wgij', vectors, theta, preferred_element_type=jnp.fl...  11.7 us
    unnamed x13, local copies, waits for them, and re-layouts  6.99 us
    dot_general x1, local copies, waits for them, and re-layouts, block_energy(): jnp.einsum('gin,wnj->wgij', vectors, theta, preferred_element_type=jnp.fl...  6.6 us
    reduce_sum x1, other arithmetic, block_energy(): traces = jnp.einsum('wgii->wg', blocks)  5.87 us
    gather x1, local copies, waits for them, and re-layouts, body(): column[source].astype(jnp.float32)  5.55 us
    select_n x1, other arithmetic, body(): jnp.where(living[:, None, None], kicked, jnp.zeros_like(kicked))  5.05 us
  transfers between devices with their start and end apart: 4, of which 4 were waited for; matrix products, arithmetic and copies ran while one was open for 25% of the time, Pallas kernels for 0%

profile of v1, /device:TPU:0, one launch (start us, length us, event | category | flops | bytes accessed | tf_op | source)
XLA Modules:
  0.0 169.5 jit_solution(13644167803137013342)
XLA Ops:
  7.2 0.0 copy-start
  7.2 0.0 all-gather.2.cloned.1.call-start
  7.2 0.7 all-gather.2.cloned.1.call-update
  7.9 0.5 collective-permute-start
  8.4 20.2 %collective-permute-done = bf16[3,2048,128]{2,1,0:T(8,128)(2,1)S(1)} collective-permute-done((bf16[3,2048,128]{2,1,0:T(8,128)(2,1)}, bf16[3,2048,128]{2,1,0:T(8,128)(2,1)S(1)}, u32[]{:S(2)}, u32[]{:S(2)}) %collective-permute-start) | collective-permute-done | bytes 1572896 | tf_op jit(solution)/shard_map/ppermute | solution.py:39
  28.6 0.0 collective-permute-start.1
  28.7 19.9 %collective-permute-done.1 = bf16[3,2048,128]{2,1,0:T(8,128)(2,1)} collective-permute-done((bf16[3,2048,128]{2,1,0:T(8,128)(2,1)S(1)}, bf16[3,2048,128]{2,1,0:T(8,128)(2,1)}, u32[]{:S(2)}, u32[]{:S(2)}) %collective-permute-start.1) | collective-permute-done | bytes 1572896 | tf_op jit(solution)/shard_map/ppermute | solution.py:39
  48.6 0.0 collective-permute-start.2
  48.6 0.9 exp.3
  49.5 0.7 broadcast_maximum_fusion
  50.1 0.6 iota_compare_fusion.1
  50.8 0.6 fusion.15
  51.4 0.7 fusion.16
  52.0 0.7 broadcast_compare_fusion
  52.7 16.1 %collective-permute-done.2 = bf16[3,2048,128]{2,1,0:T(8,128)(2,1)} collective-permute-done((bf16[3,2048,128]{2,1,0:T(8,128)(2,1)}, bf16[3,2048,128]{2,1,0:T(8,128)(2,1)}, u32[]{:S(2)}, u32[]{:S(2)}) %collective-permute-start.2) | collective-permute-done | bytes 1572896 | tf_op jit(solution)/shard_map/ppermute | solution.py:39
  68.8 1.5 constant_dynamic-update-slice_fusion.7
  70.3 1.6 constant_dynamic-update-slice_fusion.6
  71.9 0.2 constant_dynamic-update-slice_fusion.5
  72.1 0.0 copy-done
  72.1 0.2 constant_dynamic-update-slice_fusion.4
  72.3 1.6 constant_dynamic-update-slice_fusion.3
  73.9 1.6 constant_dynamic-update-slice_fusion.2
  75.6 0.2 constant_dynamic-update-slice_fusion.1
  75.8 0.2 constant_dynamic-update-slice_fusion
  76.0 3.1 %constant_dynamic-slice_fusion = bf16[12,2048,128]{2,1,0:T(8,128)(2,1)} fusion(bf16[24,2048,128]{2,1,0:T(8,128)(2,1)S(1)} %constant_dynamic-update-slice_fusion, s32[]{:T(128)S(6)} %select_n.30), kind=kLoop, calls=%fused_computation.44 | loop fusion | bytes 12582916 | tf_op jit(solution)/shard_map/jit(_roll_dynamic)/dynamic_slice | solution.py:40
  79.1 5.6 %gather_fusion = bf16[6,2048,128]{2,1,0:T(8,128)(2,1)} fusion(bf16[12,2048,128]{2,1,0:T(8,128)(2,1)} %constant_dynamic-slice_fusion, s32[1024]{0:T(1024)S(1)} %pad_clamp_fusion), kind=kCustom, calls=%fused_computation | custom fusion | bytes 6291480 | tf_op jit(solution)/shard_map/gather | solution.py:45
  84.7 5.1 %broadcast_select_fusion = (bf16[6,2048,128]{2,1,0:T(8,128)(2,1)}, bf16[6,2048,128]{2,1,0:T(8,128)(2,1)S(1)}) fusion(pred[6]{0:T(512)(128)(4,1)S(1)} %broadcast_compare_fusion, bf16[6,2048,128]{2,1,0:T(8,128)(2,1)} %gather_fusion, f32[6,2048]{1,0:T(8,128)S(1)} %exp.3), kind=kLoop, calls=%fused_computation.11 | loop fusion | flops 6291456 | bytes 9486342 | tf_op jit(solution)/shard_map/jit(_where)/select_n | solution.py:46
  89.8 4.7 %copy.17 = f32[6,128,128]{0,2,1:T(8,128)} copy(f32[6,128,128]{2,1,0:T(8,128)S(1)} %slice_convert_fusion) | data formatting | bytes 786432 | tf_op jit(solution)/shard_map/slice | solution.py:12
  94.5 1.8 %gather_fusion.1 = f32[128,6]{1,0:T(8,128)S(1)} fusion(f32[6,128,128]{0,2,1:T(8,128)} %copy.17, s32[128]{0:T(128)S(1)} %or_bitcast_fusion), kind=kCustom, calls=%fused_computation.1 | custom fusion | bytes 7168 | tf_op jit(solution)/shard_map/jit(diagonal)/gather | solution.py:14
  96.3 0.1 copy.18
  96.3 1.3 convolution_subtract_fusion.2
  97.6 1.4 fusion.5
  99.0 1.2 convolution_subtract_fusion.1
  100.2 0.5 fusion.17
  100.7 1.2 convolution_subtract_fusion
  101.9 0.5 fusion.18
  102.4 4.0 %convolution_convert_fusion = bf16[6,2048,128]{2,1,0:T(8,128)(2,1)} fusion(bf16[6,2048,128]{2,1,0:T(8,128)(2,1)S(1)} %get-tuple-element.7, f32[6,128,128]{2,1,0:T(8,128)S(1)} %fusion.18), kind=kOutput, calls=%fused_computation.9 | convolution fusion | flops 2417491968 | bytes 6684672 | tf_op jit(solution)/shard_map/wnk,wkj->wnj/dot_general | solution.py:24
  106.4 31.4 %all-gather.2.cloned.1.call-done = bf16[16,128,2048]{2,1,0:T(8,128)(2,1)} async-done(((bf16[2,128,2048]{2,1,0:T(8,128)(2,1)}), bf16[16,128,2048]{2,1,0:T(8,128)(2,1)}) %all-gather.2.cloned.1.call-update) | async-done | bytes 8388624 | tf_op jit(solution)/shard_map/all_gather | solution.py:49
  137.8 11.7 %fusion = f32[6,128,16,128]{3,1,2,0:T(8,128)} fusion(bf16[16,128,2048]{2,1,0:T(8,128)(2,1)} %all-gather.2.cloned.1.call-done, bf16[6,2048,128]{2,1,0:T(8,128)(2,1)} %convolution_convert_fusion), kind=kOutput, calls=%fused_computation.2 | convolution fusion | flops 6442450944 | bytes 17825792 | tf_op jit(solution)/shard_map/gin,wnj->wgij/dot_general | solution.py:29
  149.5 0.0 copy-start.1
  149.5 6.6 %copy.20 = f32[6,128,16,128]{1,3,2,0:T(8,128)} copy(f32[6,128,16,128]{3,1,2,0:T(8,128)} %fusion) | data formatting | bytes 12582912 | tf_op jit(solution)/shard_map/gin,wnj->wgij/dot_general | solution.py:29
  156.1 0.0 copy-done.1
  156.1 0.0 copy-start.2
  156.1 5.9 %fusion.3 = (f32[6,16]{1,0:T(8,128)S(1)}, f32[6,16]{1,0:T(8,128)S(1)}) fusion(f32[6,128,16,128]{1,3,2,0:T(8,128)} %copy.20, pred[128,128]{1,0:T(8,128)(4,1)S(1)} %copy-done.1, f32[6,128,16,128]{3,1,2,0:T(8,128)} %fusion), kind=kLoop, calls=%fused_computation.7 | loop fusion | flops 6291264 | bytes 12600064 | tf_op jit(solution)/shard_map/wgii->wg/reduce_sum | solution.py:30
  162.0 0.1 subtract_reduce_fusion
  162.1 0.0 copy-done.2
  162.1 0.5 multiply_select_fusion
  (3 shorter events, 0.0 us)
Async XLA Ops:
  7.2 64.9 %copy-start = (bf16[3,2048,128]{2,1,0:T(8,128)(2,1)S(1)}, bf16[3,2048,128]{2,1,0:T(8,128)(2,1)}, u32[]{:S(2)}) copy-start(bf16[3,2048,128]{2,1,0:T(8,128)(2,1)} %param.4) | copy-start | bytes 4718596
  7.2 130.6 %all-gather.2.cloned.1.call-start = ((), (), s32[]{:S(2)}) async-start(), calls=%async_computation | async-start | bytes 9437184 | tf_op jit(solution)/shard_map/all_gather | solution.py:49
  7.9 20.7 %collective-permute-start = (bf16[3,2048,128]{2,1,0:T(8,128)(2,1)}, bf16[3,2048,128]{2,1,0:T(8,128)(2,1)S(1)}, u32[]{:S(2)}, u32[]{:S(2)}) collective-permute-start(bf16[3,2048,128]{2,1,0:T(8,128)(2,1)} %param.4), channel_id=1, source_target_pairs={{0,8},{8,16},{16,24},{24,0},{1,9},{9,17},{17,25},{25,1},{2,10},{10... | collective-permute-start | bytes 4718600 | tf_op jit(solution)/shard_map/ppermute | solution.py:39
  28.6 19.9 %collective-permute-start.1 = (bf16[3,2048,128]{2,1,0:T(8,128)(2,1)S(1)}, bf16[3,2048,128]{2,1,0:T(8,128)(2,1)}, u32[]{:S(2)}, u32[]{:S(2)}) collective-permute-start(bf16[3,2048,128]{2,1,0:T(8,128)(2,1)S(1)} %collective-permute-done), channel_id=1, source_target_pairs={{0,8},{8,16},{16,24},{24,0},{1,9},{9,17},{17,25},{25,1},{2,10},{10... | collective-permute-start | bytes 4718600 | tf_op jit(solution)/shard_map/ppermute | solution.py:39
  48.6 20.2 %collective-permute-start.2 = (bf16[3,2048,128]{2,1,0:T(8,128)(2,1)}, bf16[3,2048,128]{2,1,0:T(8,128)(2,1)}, u32[]{:S(2)}, u32[]{:S(2)}) collective-permute-start(bf16[3,2048,128]{2,1,0:T(8,128)(2,1)} %collective-permute-done.1), channel_id=1, source_target_pairs={{0,8},{8,16},{16,24},{24,0},{1,9},{9,17},{17,25},{25,1},{2,10},{10... | collective-permute-start | bytes 4718600 | tf_op jit(solution)/shard_map/ppermute | solution.py:39
  149.5 6.6 %copy-start.1 = (pred[128,128]{1,0:T(8,128)(4,1)S(1)}, pred[128,128]{1,0:T(8,128)(4,1)}, u32[]{:S(2)}) copy-start(pred[128,128]{1,0:T(8,128)(4,1)} %iota_compare_fusion.1) | copy-start | bytes 49156
  156.1 6.0 %copy-start.2 = (s32[6]{0:T(128)S(1)}, s32[6]{0:T(128)}, u32[]{:S(2)}) copy-start(s32[6]{0:T(128)} %param.6) | copy-start | bytes 76
Sparse Core Ops, SparseCore 0:
  10.1 127.6 all-gather.1
